TPU v7x, 256 devices: a whole 4x4x8 slice. The times are simulated.
256 devices in a mesh: seq: 64 (over x, z_lo, y, core), mp: 4 (over z_hi).
Axes of the slice: x: 4, y: 4, z: 8 (z_hi: 4, z_lo: 2; z = z_hi * 2 + z_lo), core: 2. Of those that a mesh axis runs over, the one named last changes fastest.
Arguments:
- tokens: bfloat16 [8192, 4096], P('seq', 'mp'), may hold values from -6 to 6
- w_proj: bfloat16 [4096, 3, 2048], P('seq', None, 'mp'), may hold values from -0.09375 to 0.09375
- short_filter: float32 [3, 3, 2048], P(None, None, 'mp'), may hold values from -3.5 to 3.5
- long_filter: float32 [2048, 8192], P(('mp', 'seq')), may hold values from -0.0625 to 0.0625
- skip_gain: float32 [2048], P('mp'), may hold values from -4 to 4
Outputs:
- gated: bfloat16 [8192, 2048], P('seq', 'mp')
All inputs are finite; a program needn't handle non-finite values.
Results may differ from a plain program's by a relative error of at most 0.012.
Values may be sent and summed in bfloat16 or wider, within the bound.
No kernel may reach another device: no remote copies, remote signals or barrier semaphores. Data moves between devices by JAX's collectives and lax.ppermute only.
A program may use at most 64 MiB of HBM per device.

v0:
```python
import math
import jax
import jax.numpy as jnp
from jax import lax
from jax.sharding import PartitionSpec as P


def shifted(value, axis, steps):
    count = lax.axis_size(axis)
    leading, last = (max(0, -steps), min(count, count - steps))
    return lax.ppermute(value, axis, [(source, source + steps) for source in range(leading, last)])


def transform(real_part, imag_part, orient, filled):
    length = real_part.shape[-1]
    first = math.gcd(length, 64)
    highest = lax.Precision.HIGHEST
    if length <= 64 or first == 1:
        counter = jnp.arange(length, dtype=jnp.int32)
        angles = (
            2.0
            * math.pi
            / length
            * (counter[:, None] * counter[None, :] % length).astype(jnp.float32)
        )
        cosine = jnp.cos(angles)
        sine = jnp.sin(angles)
        new_real = jnp.dot(real_part, cosine, precision=highest) - orient * jnp.dot(
            imag_part, sine, precision=highest
        )
        new_imag = jnp.dot(imag_part, cosine, precision=highest) + orient * jnp.dot(
            real_part, sine, precision=highest
        )
        return (new_real, new_imag)
    second = length // first
    outer = real_part.shape[:-1]
    live = first
    if filled > 0 and filled % second == 0:
        live = filled // second
    real_grid = real_part.reshape(outer + (first, second))[..., :live, :]
    imag_grid = imag_part.reshape(outer + (first, second))[..., :live, :]
    counter = jnp.arange(first, dtype=jnp.int32)
    angles = (
        2.0 * math.pi / first * (counter[:, None] * counter[None, :] % first).astype(jnp.float32)
    )
    cosine = jnp.cos(angles)[:live]
    sine = jnp.sin(angles)[:live]
    section_real = jnp.einsum(
        "...ab,ak->...kb", real_grid, cosine, precision=highest
    ) - orient * jnp.einsum("...ab,ak->...kb", imag_grid, sine, precision=highest)
    section_imag = jnp.einsum(
        "...ab,ak->...kb", imag_grid, cosine, precision=highest
    ) + orient * jnp.einsum("...ab,ak->...kb", real_grid, sine, precision=highest)
    freq_rows = jnp.arange(first, dtype=jnp.int32)[:, None]
    time_cols = jnp.arange(second, dtype=jnp.int32)[None, :]
    twiddle = 2.0 * math.pi / length * (freq_rows * time_cols).astype(jnp.float32)
    twist_cos = jnp.cos(twiddle)
    twist_sin = jnp.sin(twiddle)
    turned_real = section_real * twist_cos - orient * section_imag * twist_sin
    turned_imag = section_imag * twist_cos + orient * section_real * twist_sin
    inner_real, inner_imag = transform(turned_real, turned_imag, orient, 0)
    final_real = jnp.swapaxes(inner_real, -1, -2).reshape(outer + (length,))
    final_imag = jnp.swapaxes(inner_imag, -1, -2).reshape(outer + (length,))
    return (final_real, final_imag)


def mirrored(values):
    return jnp.concatenate([values[:, :1], values[:, :0:-1]], axis=1)


def long_conv(signal, kernel):
    seq_len = signal.shape[-1]
    padded_signal = jnp.pad(signal.astype(jnp.float32), ((0, 0), (0, seq_len)))
    padded_kernel = jnp.pad(kernel, ((0, 0), (0, seq_len)))
    joint_real, joint_imag = transform(padded_signal, padded_kernel, -1.0, seq_len)
    mirror_real = mirrored(joint_real)
    mirror_imag = mirrored(joint_imag)
    signal_real = 0.5 * (joint_real + mirror_real)
    signal_imag = 0.5 * (joint_imag - mirror_imag)
    kernel_real = 0.5 * (joint_imag + mirror_imag)
    kernel_imag = -0.5 * (joint_real - mirror_real)
    prod_real = signal_real * kernel_real - signal_imag * kernel_imag
    prod_imag = signal_real * kernel_imag + signal_imag * kernel_real
    back_real, back_imag = transform(prod_real, prod_imag, 1.0, 0)
    return back_real[:, :seq_len] / (2.0 * seq_len)


def on_device(tokens, w_proj, short_filter, long_filter, skip_gain):
    rows_dev = tokens.shape[0]
    margin = short_filter.shape[1] - 1
    width = w_proj.shape[2]
    source = lax.all_gather(tokens, "mp", axis=1, tiled=True)
    projected = jnp.einsum(
        "td,dpc->tpc",
        source,
        lax.all_gather(w_proj, "seq", axis=0, tiled=True),
        preferred_element_type=jnp.float32,
    ).astype(jnp.bfloat16)
    tail = shifted(projected[rows_dev - margin :], "seq", 1)
    extended = jnp.concatenate([tail, projected], axis=0).astype(jnp.float32)
    mixed = jnp.zeros((rows_dev, 3, width), jnp.float32)
    for offset in range(margin + 1):
        mixed = (
            mixed
            + short_filter[:, offset, :][None]
            * extended[margin - offset : margin - offset + rows_dev]
        )
    query_rows = mixed[:, 0]
    product = (mixed[:, 1] * mixed[:, 2]).astype(jnp.bfloat16)
    groups = lax.axis_size("seq")
    channel_count = width // groups
    outgoing = product.reshape(rows_dev, groups, channel_count).transpose(1, 2, 0)
    arrived = lax.all_to_all(outgoing, "seq", split_axis=0, concat_axis=2, tiled=True)[0]
    convolved = long_conv(arrived, long_filter).astype(jnp.bfloat16)[None]
    returned = lax.all_to_all(convolved, "seq", split_axis=2, concat_axis=0, tiled=True)
    back_rows = returned.transpose(2, 0, 1).reshape(rows_dev, width)
    result = query_rows * (
        back_rows.astype(jnp.float32) + skip_gain[None, :] * product.astype(jnp.float32)
    )
    return result.astype(jnp.bfloat16)


def solution(mesh):
    return jax.shard_map(
        on_device,
        mesh=mesh,
        in_specs=(
            P("seq", "mp"),
            P("seq", None, "mp"),
            P(None, None, "mp"),
            P(("mp", "seq"), None),
            P("mp"),
        ),
        out_specs=P("seq", "mp"),
        check_vma=False,
    )
```

profile of v0, /device:TPU:1, one launch (start us, length us, event | category | flops | bytes accessed | tf_op | source)
XLA Modules:
  0.0 374.8 jit_solution(6726618726081883636)
XLA Ops:
  9.7 37.3 %all-gather.3.cloned.1.call-done = bf16[128,4096]{1,0:T(8,128)(2,1)} async-done(((bf16[128,1024]{1,0:T(8,128)(2,1)}), bf16[128,4096]{1,0:T(8,128)(2,1)}) %all-gather.3.cloned.1.call-update) | async-done | bytes 1048592 | tf_op jit(solution)/shard_map/all_gather | solution.py:92
  47.0 120.2 %all-gather.5.cloned.1.call-done = bf16[4096,3,512]{2,0,1:T(8,128)(2,1)} async-done(((bf16[64,3,512]{2,0,1:T(8,128)(2,1)}), bf16[4096,3,512]{2,0,1:T(8,128)(2,1)}) %all-gather.5.cloned.1.call-update) | async-done | bytes 12582928 | tf_op jit(solution)/shard_map/all_gather | solution.py:96
  167.2 6.7 %convolution_convert_fusion = bf16[128,3,512]{2,0,1:T(8,128)(2,1)S(1)} fusion(bf16[4096,3,512]{2,0,1:T(8,128)(2,1)} %all-gather.5.cloned.1.call-done, bf16[128,4096]{1,0:T(8,128)(2,1)} %all-gather.3.cloned.1.call-done), kind=kOutput, calls=%fused_computation.14 | convolution fusion | flops 1610809344 | bytes 14024704 | tf_op jit(solution)/shard_map/td,dpc->tpc/dot_general | solution.py:93
  173.9 2.8 collective-permute-start
  179.5 8.7 %all-to-all-start = ((bf16[64,8,128]{2,1,0:T(8,128)(2,1)}), bf16[64,8,128]{2,1,0:T(8,128)(2,1)S(1)}, u32[]{:S(2)}, u32[]{:S(2)}) async-start(bf16[64,8,128]{2,1,0:T(8,128)(2,1)} %bitcast.7), calls=%async_computation | async-start | bytes 262144 | tf_op jit(solution)/shard_map/all_to_all | solution.py:113
  189.1 7.4 %all-to-all-done = bf16[64,8,128]{2,1,0:T(8,128)(2,1)S(1)} async-done(((bf16[64,8,128]{2,1,0:T(8,128)(2,1)}), bf16[64,8,128]{2,1,0:T(8,128)(2,1)S(1)}, u32[]{:S(2)}, u32[]{:S(2)}) %all-to-all-start) | async-done | bytes 131104 | tf_op jit(solution)/shard_map/all_to_all | solution.py:113
  199.3 3.3 fusion.41
  205.7 3.3 fusion.43
  209.0 3.3 fusion.5
  212.3 4.7 %add_bitcast_fusion.1 = (f32[8,64,64,4]{1,2,3,0:T(8,128)}, f32[8,64,64,4]{1,2,3,0:T(8,128)S(1)}) fusion(f32[64,8,64,4]{2,0,3,1:T(8,128)S(1)} %fusion.5, f32[64,4]{0,1:T(4,128)S(1)} %get-tuple-element.23, f32[64,4]{0,1:T(4,128)S(1)} %get-tuple-element.22, f32[64,8,64,4]{2,0,3,1:T(8,128)S(1)} %fusion.43, f32[8,64,64,4]{2,1,3,0:T(8,128)S(1)} %copy.114), kind=kOutput, calls=%fused_computation.24 | convolution fusion | flops 101769216 | bytes 2623488 | tf_op jit(solution)/shard_map/...ab,ak->...kb/dot_general | solution.py:50
  220.9 3.1 fusion.4
  231.0 2.1 fusion.2
  234.4 8.9 %reverse = f32[8,16384]{1,0:T(8,128)S(1)} reverse(f32[8,16384]{1,0:T(8,128)S(1)} %bitcast.226), dimensions={1} | reverse | bytes 1048576
  243.5 9.3 %reverse.1 = f32[8,16384]{1,0:T(8,128)S(1)} reverse(f32[8,16384]{1,0:T(8,128)S(1)} %bitcast.229), dimensions={1} | reverse | bytes 1048576
  258.1 3.3 fusion.39
  264.5 3.3 fusion.45
  267.8 3.3 convolution_add_fusion
  271.1 4.6 %add_bitcast_fusion = (f32[8,64,64,4]{1,2,3,0:T(8,128)S(1)}, f32[8,64,64,4]{1,2,3,0:T(8,128)}) fusion(f32[64,8,64,4]{2,0,3,1:T(8,128)S(1)} %convolution_add_fusion, f32[64,4]{0,1:T(4,128)S(1)} %fusion.76, f32[64,4]{0,1:T(4,128)S(1)} %get-tuple-element.22, f32[64,8,64,4]{2,0,3,1:T(8,128)S(1)} %fusion.45, f32[8,64,64,4]{2,1,3,0:T(8,128)S(1)} %copy.134), kind=kOutput, calls=%fused_computation.22 | convolution fusion | flops 101638144 | bytes 2623488 | tf_op jit(solution)/shard_map/...ab,ak->...kb/dot_general | solution.py:50
  282.4 6.8 %copy.142 = bf16[1,8,8192]{1,0,2:T(2,128)(2,1)} copy(bf16[1,8,8192]{2,1,0:T(8,128)(2,1)S(1)} %fusion.21) | data formatting | bytes 262144 | tf_op jit(solution)/shard_map/broadcast_in_dim | solution.py:114
  289.7 45.4 %reduce = bf16[8192,8]{1,0:T(8,128)(2,1)S(1)} reduce(bf16[8192,1,8]{2,1,0:T(2,128)(2,1)} %bitcast.215, bf16[]{:T(256)} %broadcast.303), dimensions={1}, to_apply=%bitcast.180.reduce_sub_computation | reduce | bytes 262146
  335.1 2.3 reshape.159
  337.4 12.7 %all_to_all.21 = bf16[64,2,512]{2,1,0:T(2,128)(2,1)S(1)} all-to-all(bf16[64,2,512]{2,1,0:T(2,128)(2,1)S(1)} %reshape.159), channel_id=1, replica_groups=mesh['seq'=64,'mp'=4] {'seq'}, dimensions={0} | all-to-all | bytes 262144 | tf_op jit(solution)/shard_map/all_to_all | solution.py:115
  350.1 8.7 %reshape.160 = bf16[8192,1,8]{2,1,0:T(2,128)(2,1)} reshape(bf16[64,2,512]{2,1,0:T(2,128)(2,1)S(1)} %all_to_all.21) | data formatting | bytes 262144
  358.8 7.8 %copy.143 = bf16[1,8,8192]{2,1,0:T(8,128)(2,1)S(1)} copy(bf16[1,8,8192]{1,0,2:T(2,128)(2,1)} %bitcast.216) | data formatting | bytes 262144 | tf_op jit(solution)/shard_map/all_to_all | solution.py:115
  (82 shorter events, 41.7 us)
Async XLA Ops:
  6.5 181.7 %copy-start.3 = (f32[8,8192]{1,0:T(8,128)S(1)}, f32[8,8192]{1,0:T(8,128)}, u32[]{:S(2)}) copy-start(f32[8,8192]{1,0:T(8,128)} %param.8) | copy-start | bytes 786436
  6.5 40.4 %all-gather.3.cloned.1.call-start = ((), (), s32[]{:S(2)}) async-start(), calls=%async_computation.2 | async-start | bytes 1310720 | tf_op jit(solution)/shard_map/all_gather | solution.py:92
  7.3 159.9 %all-gather.5.cloned.1.call-start = ((), (), s32[]{:S(2)}) async-start(), calls=%async_computation.3 | async-start | bytes 12779520 | tf_op jit(solution)/shard_map/all_gather | solution.py:96
  173.9 3.6 collective-permute-start
  177.8 0.9 copy-start
  179.5 17.0 %all-to-all-start = ((bf16[64,8,128]{2,1,0:T(8,128)(2,1)}), bf16[64,8,128]{2,1,0:T(8,128)(2,1)S(1)}, u32[]{:S(2)}, u32[]{:S(2)}) async-start(bf16[64,8,128]{2,1,0:T(8,128)(2,1)} %bitcast.7), calls=%async_computation | async-start | bytes 262144 | tf_op jit(solution)/shard_map/all_to_all | solution.py:113
  227.8 25.2 %slice-start = ((f32[8,16384]{1,0:T(8,128)}), f32[8,1]{1,0:T(8,128)S(1)}, s32[]{:S(2)}) async-start(f32[8,16384]{1,0:T(8,128)} %reshape.130), calls=%async_computation.4 | async-start | bytes 8192 | tf_op jit(solution)/shard_map/slice | solution.py:68
  227.8 25.6 %copy-start.2 = (f32[8,64,256]{2,1,0:T(8,128)S(1)}, f32[8,64,256]{2,1,0:T(8,128)}, u32[]{:S(2)}) copy-start(f32[8,64,256]{2,1,0:T(8,128)} %reshape.129) | copy-start | bytes 1572868
  282.0 85.0 %copy-start.1 = (f32[128,3,512]{2,0,1:T(8,128)S(1)}, f32[128,3,512]{2,0,1:T(8,128)}, u32[]{:S(2)}) copy-start(f32[128,3,512]{2,0,1:T(8,128)} %copy-done) | copy-start | bytes 2359300
  282.0 85.0 %copy-start.4 = (f32[512]{0:T(512)S(1)}, f32[512]{0:T(512)}, u32[]{:S(2)}) copy-start(f32[512]{0:T(512)} %param.9) | copy-start | bytes 6148
Sparse Core Ops, SparseCore 0:
  9.1 37.7 all-gather.2
  48.8 118.2 all-gather.4
where the time goes:
time: 379 us; the launch traced here: 375 us
  waiting for transfers between devices  167 us (44%)
  local copies, waits for them, and re-layouts  67.2 us (18%)
  matrix products  54 us (14%)
  other arithmetic  48.3 us (13%)
  between operations  14.1 us (4%)
  blocking collectives  12.7 us (3%)
  starting transfers between devices  11.5 us (3%)
    all_gather x1, waiting for transfers between devices, on_device(): lax.all_gather(w_proj, 'seq', axis=0, tiled=True)  120 us
    unnamed x2, other arithmetic  45.4 us
    all_gather x1, waiting for transfers between devices, on_device(): source = lax.all_gather(tokens, 'mp', axis=1, tiled=True)  37.3 us
    unnamed x22, local copies, waits for them, and re-layouts  31.3 us
    all_to_all x1, blocking collectives, on_device(): lax.all_to_all(convolved, 'seq', split_axis=2, concat_axis=0, tiled=True)  12.7 us
    dot_general x4, matrix products, transform(): jnp.einsum('...ab,ak->...kb', imag_grid, sine, precision=highest)  10.8 us
    all_to_all x1, starting transfers between devices, on_device(): lax.all_to_all(outgoing, 'seq', split_axis=0, concat_axis=2, tiled=True)[0]  8.66 us
    dot_general x4, matrix products, transform(): jnp.einsum('...ab,ak->...kb', imag_grid, cosine, precision=highest)  7.92 us
  transfers between devices with their start and end apart: 4, of which 4 were waited for; matrix products, arithmetic and copies ran while one was open for 1% of the time, Pallas kernels for 0%

commit v1 on v0

--- a/solution.py
+++ b/solution.py
@@ -89,7 +89,9 @@
     rows_dev = tokens.shape[0]
     margin = short_filter.shape[1] - 1
     width = w_proj.shape[2]
-    source = lax.all_gather(tokens, "mp", axis=1, tiled=True)
+    source = jnp.concatenate(
+        lax.all_to_all(jnp.stack([tokens] * lax.axis_size("mp")), "mp", 0, 0), axis=1
+    )
     projected = jnp.einsum(
         "td,dpc->tpc",
         source,

time: 379 us -> 355 us (0.937)
  waiting for transfers between devices: 167 us -> 129 us
  starting transfers between devices: 11.5 us -> 20.6 us
    all_gather x1 -> x0, waiting for transfers between devices: 37.3 us -> none  [on_device(): source = lax.all_gather(tokens, 'mp', axis=1, tiled=True)]
    all_to_all x0 -> x1, waiting for transfers between devices: none -> 29.7 us  [on_device(): lax.all_to_all(jnp.stack([tokens] * lax.axis_size('mp')), 'mp', 0, 0)]
    all_gather x1, waiting for transfers between devices: 120 us -> 90.9 us  [on_device(): lax.all_gather(w_proj, 'seq', axis=0, tiled=True)]
    all_to_all x0 -> x1, starting transfers between devices: none -> 9 us  [on_device(): lax.all_to_all(jnp.stack([tokens] * lax.axis_size('mp')), 'mp', 0, 0)]
  transfers between devices with their start and end apart: 4 -> 4, of which waited for: 4 -> 4; matrix products, arithmetic and copies ran while one was open for 1% -> 2% of each run, Pallas kernels for 0% -> 0%
where the time goes in v1:
time: 355 us; the launch traced here: 350 us
  waiting for transfers between devices  129 us (36%)
  local copies, waits for them, and re-layouts  70.8 us (20%)
  matrix products  53.6 us (15%)
  other arithmetic  48.3 us (14%)
  starting transfers between devices  20.6 us (6%)
  between operations  14.1 us (4%)
  blocking collectives  12.7 us (4%)
    all_gather x1, waiting for transfers between devices, on_device(): lax.all_gather(w_proj, 'seq', axis=0, tiled=True)  90.9 us
    unnamed x2, other arithmetic  45.4 us
    unnamed x22, local copies, waits for them, and re-layouts  31.2 us
    all_to_all x1, waiting for transfers between devices, on_device(): lax.all_to_all(jnp.stack([tokens] * lax.axis_size('mp')), 'mp', 0, 0)  29.7 us
    all_to_all x1, blocking collectives, on_device(): lax.all_to_all(convolved, 'seq', split_axis=2, concat_axis=0, tiled=True)  12.7 us
    dot_general x4, matrix products, transform(): jnp.einsum('...ab,ak->...kb', imag_grid, sine, precision=highest)  10.8 us
    all_to_all x1, starting transfers between devices, on_device(): lax.all_to_all(jnp.stack([tokens] * lax.axis_size('mp')), 'mp', 0, 0)  9 us
    all_to_all x1, starting transfers between devices, on_device(): lax.all_to_all(outgoing, 'seq', split_axis=0, concat_axis=2, tiled=True)[0]  8.84 us
  transfers between devices with their start and end apart: 4, of which 4 were waited for; matrix products, arithmetic and copies ran while one was open for 2% of the time, Pallas kernels for 0%

profile of v1, /device:TPU:1, one launch (start us, length us, event | category | flops | bytes accessed | tf_op | source)
XLA Modules:
  0.0 349.5 jit_solution(3642615324121616489)
XLA Ops:
  9.4 9.0 %all-to-all-start = ((bf16[4,128,1024]{2,1,0:T(8,128)(2,1)}), bf16[4,128,1024]{2,1,0:T(8,128)(2,1)S(1)}, u32[]{:S(2)}, u32[]{:S(2)}) async-start(bf16[4,128,1024]{2,1,0:T(8,128)(2,1)} %stack.2), calls=%async_computation | async-start | bytes 2097152 | tf_op jit(solution)/shard_map/all_to_all | solution.py:93
  20.0 29.7 %all-to-all-done = bf16[4,128,1024]{2,1,0:T(8,128)(2,1)S(1)} async-done(((bf16[4,128,1024]{2,1,0:T(8,128)(2,1)}), bf16[4,128,1024]{2,1,0:T(8,128)(2,1)S(1)}, u32[]{:S(2)}, u32[]{:S(2)}) %all-to-all-start) | async-done | bytes 1048608 | tf_op jit(solution)/shard_map/all_to_all | solution.py:93
  51.3 90.9 %all-gather.2.cloned.1.call-done = bf16[4096,3,512]{2,0,1:T(8,128)(2,1)} async-done(((bf16[64,3,512]{2,0,1:T(8,128)(2,1)}), bf16[4096,3,512]{2,0,1:T(8,128)(2,1)}) %all-gather.2.cloned.1.call-update) | async-done | bytes 12582928 | tf_op jit(solution)/shard_map/all_gather | solution.py:98
  142.2 6.4 %convolution_convert_fusion = bf16[128,3,512]{2,0,1:T(8,128)(2,1)S(1)} fusion(bf16[128,4096,1]{1,0,2:T(8,128)(2,1)S(1)} %reshape.152, bf16[4096,3,512]{2,0,1:T(8,128)(2,1)} %all-gather.2.cloned.1.call-done), kind=kOutput, calls=%fused_computation.14 | convolution fusion | flops 1610809344 | bytes 14024704 | tf_op jit(solution)/shard_map/td,dpc->tpc/dot_general | solution.py:95
  148.6 2.8 collective-permute-start
  154.2 8.8 %all-to-all-start.1 = ((bf16[64,8,128]{2,1,0:T(8,128)(2,1)}), bf16[64,8,128]{2,1,0:T(8,128)(2,1)S(1)}, u32[]{:S(2)}, u32[]{:S(2)}) async-start(bf16[64,8,128]{2,1,0:T(8,128)(2,1)} %bitcast.7), calls=%async_computation.1 | async-start | bytes 262144 | tf_op jit(solution)/shard_map/all_to_all | solution.py:115
  164.0 7.4 %all-to-all-done.1 = bf16[64,8,128]{2,1,0:T(8,128)(2,1)S(1)} async-done(((bf16[64,8,128]{2,1,0:T(8,128)(2,1)}), bf16[64,8,128]{2,1,0:T(8,128)(2,1)S(1)}, u32[]{:S(2)}, u32[]{:S(2)}) %all-to-all-start.1) | async-done | bytes 131104 | tf_op jit(solution)/shard_map/all_to_all | solution.py:115
  174.1 3.3 fusion.40
  180.5 3.3 fusion.42
  183.8 3.3 fusion.5
  187.1 4.6 %add_bitcast_fusion.1 = (f32[8,64,64,4]{1,2,3,0:T(8,128)}, f32[8,64,64,4]{1,2,3,0:T(8,128)S(1)}) fusion(f32[64,8,64,4]{2,0,3,1:T(8,128)S(1)} %fusion.5, f32[64,4]{0,1:T(4,128)S(1)} %get-tuple-element.23, f32[64,4]{0,1:T(4,128)S(1)} %get-tuple-element.22, f32[64,8,64,4]{2,0,3,1:T(8,128)S(1)} %fusion.42, f32[8,64,64,4]{2,1,3,0:T(8,128)S(1)} %copy.116), kind=kOutput, calls=%fused_computation.23 | convolution fusion | flops 101769216 | bytes 2623488 | tf_op jit(solution)/shard_map/...ab,ak->...kb/dot_general | solution.py:50
  195.7 3.0 fusion.4
  209.2 8.9 %reverse = f32[8,16384]{1,0:T(8,128)S(1)} reverse(f32[8,16384]{1,0:T(8,128)S(1)} %bitcast.226), dimensions={1} | reverse | bytes 1048576
  218.3 9.3 %reverse.1 = f32[8,16384]{1,0:T(8,128)S(1)} reverse(f32[8,16384]{1,0:T(8,128)S(1)} %bitcast.229), dimensions={1} | reverse | bytes 1048576
  232.9 3.3 fusion.38
  239.3 3.3 fusion.44
  242.6 3.3 convolution_add_fusion
  245.9 4.6 %add_bitcast_fusion = (f32[8,64,64,4]{1,2,3,0:T(8,128)S(1)}, f32[8,64,64,4]{1,2,3,0:T(8,128)}) fusion(f32[64,8,64,4]{2,0,3,1:T(8,128)S(1)} %convolution_add_fusion, f32[64,4]{0,1:T(4,128)S(1)} %fusion.75, f32[64,4]{0,1:T(4,128)S(1)} %get-tuple-element.22, f32[64,8,64,4]{2,0,3,1:T(8,128)S(1)} %fusion.44, f32[8,64,64,4]{2,1,3,0:T(8,128)S(1)} %copy.136), kind=kOutput, calls=%fused_computation.21 | convolution fusion | flops 101638144 | bytes 2623488 | tf_op jit(solution)/shard_map/...ab,ak->...kb/dot_general | solution.py:50
  257.2 6.7 %copy.144 = bf16[1,8,8192]{1,0,2:T(2,128)(2,1)} copy(bf16[1,8,8192]{2,1,0:T(8,128)(2,1)S(1)} %fusion.20) | data formatting | bytes 262144 | tf_op jit(solution)/shard_map/broadcast_in_dim | solution.py:116
  264.4 45.4 %reduce = bf16[8192,8]{1,0:T(8,128)(2,1)S(1)} reduce(bf16[8192,1,8]{2,1,0:T(2,128)(2,1)} %bitcast.214, bf16[]{:T(256)} %broadcast.305), dimensions={1}, to_apply=%bitcast.178.reduce_sub_computation | reduce | bytes 262146
  309.9 2.3 reshape.170
  312.1 12.7 %all_to_all.26 = bf16[64,2,512]{2,1,0:T(2,128)(2,1)S(1)} all-to-all(bf16[64,2,512]{2,1,0:T(2,128)(2,1)S(1)} %reshape.170), channel_id=1, replica_groups=mesh['seq'=64,'mp'=4] {'seq'}, dimensions={0} | all-to-all | bytes 262144 | tf_op jit(solution)/shard_map/all_to_all | solution.py:117
  324.9 8.6 %reshape.171 = bf16[8192,1,8]{2,1,0:T(2,128)(2,1)} reshape(bf16[64,2,512]{2,1,0:T(2,128)(2,1)S(1)} %all_to_all.26) | data formatting | bytes 262144
  333.5 7.8 %copy.145 = bf16[1,8,8192]{2,1,0:T(8,128)(2,1)S(1)} copy(bf16[1,8,8192]{1,0,2:T(2,128)(2,1)} %bitcast.215) | data formatting | bytes 262144 | tf_op jit(solution)/shard_map/all_to_all | solution.py:117
  (84 shorter events, 46.8 us)
Async XLA Ops:
  6.5 135.7 %all-gather.2.cloned.1.call-start = ((), (), s32[]{:S(2)}) async-start(), calls=%async_computation.3 | async-start | bytes 12779520 | tf_op jit(solution)/shard_map/all_gather | solution.py:98
  9.4 40.3 %all-to-all-start = ((bf16[4,128,1024]{2,1,0:T(8,128)(2,1)}), bf16[4,128,1024]{2,1,0:T(8,128)(2,1)S(1)}, u32[]{:S(2)}, u32[]{:S(2)}) async-start(bf16[4,128,1024]{2,1,0:T(8,128)(2,1)} %stack.2), calls=%async_computation | async-start | bytes 2097152 | tf_op jit(solution)/shard_map/all_to_all | solution.py:93
  18.4 144.7 %copy-start.3 = (f32[8,8192]{1,0:T(8,128)S(1)}, f32[8,8192]{1,0:T(8,128)}, u32[]{:S(2)}) copy-start(f32[8,8192]{1,0:T(8,128)} %param.8) | copy-start | bytes 786436
  148.6 3.5 %collective-permute-start = (bf16[2,3,512]{2,0,1:T(2,128)(2,1)S(1)}, bf16[2,3,512]{2,0,1:T(2,128)(2,1)S(1)}, u32[]{:S(2)}, u32[]{:S(2)}) collective-permute-start(bf16[2,3,512]{2,0,1:T(2,128)(2,1)S(1)} %slice.84), channel_id=1, source_target_pairs={{0,4},{4,8},{8,12},{12,16},{16,20},{20,24},{24,28},{28,32},{32,36}... | collective-permute-start | bytes 18440 | tf_op jit(solution)/shard_map/ppermute | solution.py:11
  152.5 0.9 copy-start
  154.2 17.2 %all-to-all-start.1 = ((bf16[64,8,128]{2,1,0:T(8,128)(2,1)}), bf16[64,8,128]{2,1,0:T(8,128)(2,1)S(1)}, u32[]{:S(2)}, u32[]{:S(2)}) async-start(bf16[64,8,128]{2,1,0:T(8,128)(2,1)} %bitcast.7), calls=%async_computation.1 | async-start | bytes 262144 | tf_op jit(solution)/shard_map/all_to_all | solution.py:115
  202.6 25.2 %slice-start = ((f32[8,16384]{1,0:T(8,128)}), f32[8,1]{1,0:T(8,128)S(1)}, s32[]{:S(2)}) async-start(f32[8,16384]{1,0:T(8,128)} %reshape.140), calls=%async_computation.4 | async-start | bytes 8192 | tf_op jit(solution)/shard_map/slice | solution.py:68
  202.6 25.6 %copy-start.2 = (f32[8,64,256]{2,1,0:T(8,128)S(1)}, f32[8,64,256]{2,1,0:T(8,128)}, u32[]{:S(2)}) copy-start(f32[8,64,256]{2,1,0:T(8,128)} %reshape.139) | copy-start | bytes 1572868
  256.8 84.9 %copy-start.1 = (f32[128,3,512]{2,0,1:T(8,128)S(1)}, f32[128,3,512]{2,0,1:T(8,128)}, u32[]{:S(2)}) copy-start(f32[128,3,512]{2,0,1:T(8,128)} %copy-done) | copy-start | bytes 2359300
  256.8 84.9 %copy-start.4 = (f32[512]{0:T(512)S(1)}, f32[512]{0:T(512)}, u32[]{:S(2)}) copy-start(f32[512]{0:T(512)} %param.9) | copy-start | bytes 6148
Sparse Core Ops, SparseCore 0:
  9.2 132.9 all-gather.1
